TPU v7x, 32 devices: a whole 2x2x4 slice. The times are simulated.
32 devices in a mesh: dp: 8 (over z, core), leaf: 4 (over y, x).
Axes of the slice: x: 2, y: 2, z: 4, core: 2. Of those that a mesh axis runs over, the one named last changes fastest.
Arguments:
- features: bfloat16 [51200, 384], P(('dp', 'leaf')), may hold values from -6 to 6
- head_weight: bfloat16 [384, 1536], replicated, may hold values from -0.3125 to 0.3125
- gain: float32 [1536], replicated, may hold values from 0.5 to 1.5
- shift: float32 [1536], replicated, may hold values from -3 to 3
- node_weights: bfloat16 [4096, 1536], P('leaf'), may hold values from -0.15625 to 0.15625
- subtree_map: int32 [64], replicated, may hold values from 0 to 63, each once
- node_ids: int32 [512, 64], P('dp'), may hold values from -1 to 4095, as said below
Outputs:
- head_grad: float32 [384, 1536], P(None, 'dp')
- gain_grad: float32 [1536], P('dp')
- shift_grad: float32 [1536], P('dp')
- node_grad: float32 [4096, 1536], P('leaf', 'dp')
Inputs may be any that keep to these rules, and one draw needn't show every extreme that they name: `node_ids`: each image has 1 to 16 positive ids, all in one subtree, in its first columns, then -1; and 1 to 48 hard-negative ids in another subtree from column 16 on, then -1. Ids of one image are distinct. The first image has full counts.
All inputs are finite; a program needn't handle non-finite values.
Results may differ from a plain program's by a relative error of at most 0.0036.
Values may be sent and summed in bfloat16 or wider, within the bound.
No kernel may reach another device: no remote copies, remote signals or barrier semaphores. Data moves between devices by JAX's collectives and lax.ppermute only.
A program may use at most 128 MiB of HBM per device.

v0:
```python
import jax
import jax.numpy as jnp
from jax import lax
from jax.sharding import PartitionSpec as P

P_SIZE = 100
SUB_SIZE = 64
KPOS = 16


def slot_table(slot_rows, owned_rows, values_rows, slots_dev):
    column = jnp.arange(slots_dev, dtype=jnp.int32)[None, None, :]
    match = (slot_rows[:, :, None] == column) & owned_rows[:, :, None]
    return jnp.sum(jnp.where(match, values_rows[:, :, None], 0.0), axis=1)


def shards(features, head_weight, gain, shift, node_weights, subtree_map, node_ids):
    images_here = features.shape[0] // P_SIZE
    width = head_weight.shape[1]
    linear_scores = jnp.dot(features, head_weight, preferred_element_type=jnp.float32)
    shifted = gain * linear_scores + shift
    sig = jax.nn.sigmoid(shifted)
    active = shifted * sig
    embedded = jnp.mean(active.reshape(images_here, P_SIZE, width), axis=1).astype(jnp.bfloat16)
    grouped = lax.all_gather(embedded, "leaf", axis=0, tiled=True)
    slots_dev = node_weights.shape[0]
    valid_pair = node_ids >= 0
    safe_ids = jnp.where(valid_pair, node_ids, 0)
    subtree = safe_ids // SUB_SIZE
    matches = (
        subtree[:, :, None] == jnp.arange(subtree_map.shape[0], dtype=jnp.int32)[None, None, :]
    )
    placed = jnp.sum(jnp.where(matches, subtree_map[None, None, :], 0), axis=2)
    slot_row = placed * SUB_SIZE + safe_ids % SUB_SIZE
    owned = valid_pair & (slot_row // slots_dev == lax.axis_index("leaf"))
    local_slot = jnp.where(owned, slot_row % slots_dev, 0)
    scores = lax.dot_general(
        grouped, node_weights, (((1,), (1,)), ((), ())), preferred_element_type=jnp.float32
    )
    target = (jnp.arange(node_ids.shape[1]) < KPOS).astype(jnp.float32)
    hit_count = slot_table(local_slot, owned, jnp.ones(local_slot.shape, jnp.float32), slots_dev)
    positive = slot_table(
        local_slot, owned, jnp.broadcast_to(target[None, :], local_slot.shape), slots_dev
    )
    table = jnp.where(hit_count > 0.5, jax.nn.sigmoid(scores) - positive, 0.0).astype(jnp.bfloat16)
    grad_part = jnp.dot(table, node_weights, preferred_element_type=jnp.float32)
    emb_grad = lax.psum_scatter(grad_part, "leaf", scatter_dimension=0, tiled=True)
    column_ids = jnp.arange(slots_dev, dtype=jnp.int32)[None, None, :]
    pick = (local_slot[:, :, None] == column_ids) & owned[:, :, None]
    coef = jnp.sum(jnp.where(pick, table.astype(jnp.float32)[:, None, :], 0.0), axis=2).astype(
        jnp.bfloat16
    )
    columns = lax.all_to_all(grouped, "dp", split_axis=1, concat_axis=0, tiled=True)
    all_coef = lax.all_gather(coef, "dp", axis=0, tiled=True)
    all_slot = lax.all_gather(local_slot, "dp", axis=0, tiled=True)
    every_pair = jnp.ones(all_slot.shape, jnp.bool_)
    all_table = slot_table(all_slot, every_pair, all_coef.astype(jnp.float32), slots_dev).astype(
        jnp.bfloat16
    )
    node_grad = lax.dot_general(
        all_table, columns, (((0,), (0,)), ((), ())), preferred_element_type=jnp.float32
    )
    slope = (sig * (1.0 + shifted * (1.0 - sig))).reshape(images_here, P_SIZE, width)
    pixel_gradient = ((emb_grad / P_SIZE)[:, None, :] * slope).reshape(images_here * P_SIZE, width)
    lin_grad = (pixel_gradient * gain).astype(jnp.bfloat16)
    head_term = lax.dot_general(
        features, lin_grad, (((0,), (0,)), ((), ())), preferred_element_type=jnp.float32
    )
    gain_term = jnp.sum(pixel_gradient * linear_scores, axis=0)
    shift_term = jnp.sum(pixel_gradient, axis=0)
    split_sums = (
        lax.psum_scatter(head_term, "dp", scatter_dimension=1, tiled=True),
        lax.psum_scatter(gain_term, "dp", scatter_dimension=0, tiled=True),
        lax.psum_scatter(shift_term, "dp", scatter_dimension=0, tiled=True),
    )
    head_grad, gain_grad, shift_grad = lax.psum(
        (split_sums[0], split_sums[1], split_sums[2]), "leaf"
    )
    return (head_grad, gain_grad, shift_grad, node_grad)


def solution(mesh):
    in_specs = (P(("dp", "leaf"), None), P(), P(), P(), P("leaf", None), P(), P("dp", None))
    out_specs = (P(None, "dp"), P("dp"), P("dp"), P("leaf", "dp"))
    return jax.shard_map(shards, mesh=mesh, in_specs=in_specs, out_specs=out_specs, check_vma=False)
```

profile of v0, /device:TPU:0, one launch (start us, length us, event | category | flops | bytes accessed | tf_op | source)
XLA Modules:
  0.0 237.6 jit_solution(990321862324019750)
XLA Ops:
  7.2 0.9 add_select_fusion.3
  8.2 11.9 %fusion.1 = (f32[1600,1536]{1,0:T(8,128)}, f32[1600,1536]{1,0:T(8,128)}) fusion(f32[1536]{0:T(1024)} %param.10, f32[1536]{0:T(1024)} %param.9, bf16[1600,384]{1,0:T(8,128)(2,1)} %param.7, bf16[384,1536]{1,0:T(8,128)(2,1)} %param.8), kind=kOutput, calls=%fused_computation.11 | convolution fusion | flops 1902182400 | bytes 22081536 | tf_op jit(solution)/shard_map/dot_general | solution.py:20
  20.1 10.0 %reshape.27 = f32[16,100,1536]{2,1,0:T(8,128)} reshape(f32[1600,1536]{1,0:T(8,128)} %get-tuple-element.15) | data formatting | bytes 19660800 | tf_op jit(solution)/shard_map/reshape | solution.py:24
  30.1 5.3 %reduce_sum.74 = f32[16,1536]{1,0:T(8,128)S(1)} reduce(f32[16,100,1536]{2,1,0:T(8,128)} %reshape.27, f32[]{:T(128)} %constant.65.clone.1), dimensions={1}, to_apply=%region_2.3 | reduce | flops 2433024 | bytes 9928708 | tf_op jit(solution)/shard_map/reduce_sum | solution.py:24
  35.5 10.2 %all_gather.9 = bf16[64,1536]{1,0:T(8,128)(2,1)S(1)} all-gather(bf16[16,1536]{1,0:T(8,128)(2,1)S(1)} %multiply_convert_fusion.4), channel_id=1, replica_groups=mesh['dp'=8,'leaf'=4] {'leaf'}, dimensions={0}, use_global_device_ids=true | all-gather | bytes 245760 | tf_op jit(solution)/shard_map/all_gather | solution.py:25
  45.6 1.8 select_reduce_fusion.4
  47.6 9.4 %select_reduce_fusion.3 = (f32[64,1024]{1,0:T(8,128)S(1)}, f32[64,1024]{1,0:T(8,128)S(1)}) fusion(s32[64,64]{1,0:T(8,128)S(1)} %get-tuple-element.13, pred[64,64]{1,0:T(8,128)(4,1)S(1)} %get-tuple-element.14, f32[64]{0:T(128)S(1)} %compare_convert_fusion), kind=kLoop, calls=%fused_computation.4 | loop fusion | flops 25034752 | bytes 545024 | tf_op jit(solution)/shard_map/reduce_sum | solution.py:14
  56.9 1.8 fusion.21
  58.7 1.4 fusion.22
  60.4 24.7 %reduce-scatter.3.cloned.1.call-done = f32[16,1536]{1,0:T(8,128)} async-done(((f32[64,1536]{1,0:T(8,128)}), f32[16,1536]{1,0:T(8,128)}) %reduce-scatter.3.cloned.1.call-update) | async-done | bytes 98320 | tf_op jit(solution)/shard_map/reduce_scatter | solution.py:47
  86.0 5.2 %mul.45 = f32[16,100,1536]{2,1,0:T(8,128)} broadcast(f32[16,1536]{1,0:T(8,128)S(1)} %broadcast_multiply_fusion), dimensions={0,2} | broadcast | bytes 9928704 | tf_op jit(solution)/shard_map/mul | solution.py:64
  91.2 10.0 %mul.46 = f32[1600,1536]{1,0:T(8,128)} reshape(f32[16,100,1536]{2,1,0:T(8,128)} %mul.45) | data formatting | bytes 19660800 | tf_op jit(solution)/shard_map/mul | solution.py:64
  101.2 9.0 %fusion.20 = (f32[1536]{0:T(1024)S(1)}, f32[1536]{0:T(1024)S(1)}, f32[1600,1536]{1,0:T(8,128)S(1)}) fusion(f32[1600,1536]{1,0:T(8,128)} %get-tuple-element.16, f32[1600,1536]{1,0:T(8,128)} %mul.46, f32[1536]{0:T(1024)S(1)} %copy-done.2, f32[1536]{0:T(1024)S(1)} %copy-done.3), kind=kLoop, calls=%fused_computation.52 | loop fusion | flops 31945728 | bytes 29515776 | tf_op jit(solution)/shard_map/reduce_sum | solution.py:70
  110.3 4.5 %fusion.4 = f32[384,1536]{0,1:T(8,128)} fusion(bf16[1600,384]{1,0:T(8,128)(2,1)S(1)} %copy-done.5, f32[1600,1536]{1,0:T(8,128)S(1)} %get-tuple-element.12, f32[1536]{0:T(1024)S(1)} %copy-done.3), kind=kOutput, calls=%fused_computation.15 | convolution fusion | flops 1892352000 | bytes 13424640 | tf_op jit(solution)/shard_map/dot_general | solution.py:66
  115.7 1.7 copy.13
  117.4 4.6 %all-to-all-start = ((bf16[64,8,192]{2,0,1:T(8,128)(2,1)}), bf16[64,8,192]{2,0,1:T(8,128)(2,1)}, u32[]{:S(2)}, u32[]{:S(2)}) async-start(bf16[64,8,192]{2,0,1:T(8,128)(2,1)} %copy.13), calls=%async_computation.2 | async-start | bytes 524288 | tf_op jit(solution)/shard_map/all_to_all | solution.py:53
  122.1 5.3 %select_reduce_fusion.1 = bf16[64,64]{1,0:T(8,128)(2,1)S(1)} fusion(f32[64,1024]{1,0:T(8,128)} %get-tuple-element.17, s32[64,64]{1,0:T(8,128)S(1)} %get-tuple-element.13, pred[64,64]{1,0:T(8,128)(4,1)S(1)} %get-tuple-element.14), kind=kLoop, calls=%fused_computation.2 | loop fusion | flops 16773120 | bytes 290816 | tf_op jit(solution)/shard_map/reduce_sum | solution.py:50
  127.4 16.8 %all_gather.11 = bf16[512,64]{1,0:T(8,128)(2,1)S(1)} all-gather(bf16[64,64]{1,0:T(8,128)(2,1)S(1)} %select_reduce_fusion.1), channel_id=1, replica_groups=mesh['dp'=8,'leaf'=4] {'dp'}, dimensions={0}, use_global_device_ids=true | all-gather | bytes 73728 | tf_op jit(solution)/shard_map/all_gather | solution.py:54
  144.3 15.8 %all_gather.10 = s32[512,64]{1,0:T(8,128)} all-gather(s32[64,64]{1,0:T(8,128)S(1)} %get-tuple-element.13), channel_id=1, replica_groups=mesh['dp'=8,'leaf'=4] {'dp'}, dimensions={0}, use_global_device_ids=true | all-gather | bytes 147456 | tf_op jit(solution)/shard_map/all_gather | solution.py:55
  160.1 28.2 %select_reduce_fusion = bf16[512,1024]{1,0:T(8,128)(2,1)} fusion(f32[512,64]{1,0:T(8,128)S(1)} %convert_element_type.30, s32[512,64]{1,0:T(8,128)} %all_gather.10), kind=kLoop, calls=%fused_computation | loop fusion | flops 100139008 | bytes 1310720 | tf_op jit(solution)/shard_map/reduce_sum | solution.py:14
  189.6 2.6 %fusion.23 = f32[1024,192]{0,1:T(8,128)} fusion(bf16[512,1024]{1,0:T(8,128)(2,1)} %select_reduce_fusion, bf16[512,192]{1,0:T(8,128)(2,1)} %bitcast.2), kind=kOutput, calls=%fused_computation.55 | convolution fusion | flops 201326592 | bytes 2031616 | tf_op jit(solution)/shard_map/dot_general | solution.py:60
  192.1 27.6 %all-reduce.2 = (f32[1536]{0:T(1024)S(1)}, f32[1536]{0:T(1024)S(1)}) all-reduce(f32[1536]{0:T(1024)S(1)} %get-tuple-element.5, f32[1536]{0:T(1024)S(1)} %get-tuple-element.4), channel_id=4, replica_groups=mesh['dp'=8,'leaf'=4] {'dp'}, use_global_device_ids=true, to_apply=%region_8.9.clone | all-reduce | flops 3072 | bytes 24576
  219.9 9.4 %all-reduce.3 = (f32[192]{0:T(256)}, f32[192]{0:T(256)}) all-reduce(f32[192]{0:T(256)S(1)} %dynamic-slice.1, f32[192]{0:T(256)S(1)} %dynamic-slice.3), channel_id=1, replica_groups=mesh['dp'=8,'leaf'=4] {'leaf'}, use_global_device_ids=true, to_apply=%region_9.10 | all-reduce | flops 384 | bytes 3072 | tf_op jit(solution)/shard_map/psum | solution.py:76
  229.4 1.7 copy.15
  (32 shorter events, 3.0 us)
Async XLA Ops:
  7.2 49.8 %copy-start = (bf16[1024,1536]{1,0:T(8,128)(2,1)S(1)}, bf16[1024,1536]{1,0:T(8,128)(2,1)}, u32[]{:S(2)}) copy-start(bf16[1024,1536]{1,0:T(8,128)(2,1)} %param.11) | copy-start | bytes 9437188
  7.2 77.9 %reduce-scatter.3.cloned.1.call-start = ((), (), s32[]{:S(2)}) async-start(), calls=%async_computation.3 | async-start | bytes 491520 | tf_op jit(solution)/shard_map/reduce_scatter | solution.py:47
  30.1 15.5 %copy-start.4 = (s32[64]{0:T(128)S(1)}, s32[64]{0:T(128)}, u32[]{:S(2)}) copy-start(s32[64]{0:T(128)} %param.12) | copy-start | bytes 772
  30.1 17.3 %copy-start.1 = (s32[64,64]{1,0:T(8,128)S(1)}, s32[64,64]{1,0:T(8,128)}, u32[]{:S(2)}) copy-start(s32[64,64]{1,0:T(8,128)} %param.13) | copy-start | bytes 49156
  60.2 99.9 %reduce-scatter.5.cloned.1.call-start = ((), (), s32[]{:S(2)}) async-start(), calls=%async_computation.4 | async-start | bytes 2654208 | tf_op jit(solution)/shard_map/reduce_scatter | solution.py:72
  91.1 10.1 %copy-start.2 = (f32[1536]{0:T(1024)S(1)}, f32[1536]{0:T(1024)}, u32[]{:S(2)}) copy-start(f32[1536]{0:T(1024)} %param.10) | copy-start | bytes 18436
  91.2 10.1 %copy-start.3 = (f32[1536]{0:T(1024)S(1)}, f32[1536]{0:T(1024)}, u32[]{:S(2)}) copy-start(f32[1536]{0:T(1024)} %param.9) | copy-start | bytes 18436
  101.2 9.0 %copy-start.5 = (bf16[1600,384]{1,0:T(8,128)(2,1)S(1)}, bf16[1600,384]{1,0:T(8,128)(2,1)}, u32[]{:S(2)}) copy-start(bf16[1600,384]{1,0:T(8,128)(2,1)} %param.7) | copy-start | bytes 3686404
  110.3 78.1 %copy-start.6 = (u32[32]{0:T(128)S(1)}, u32[32]{0:T(128)}, u32[]{:S(2)}) copy-start(u32[32]{0:T(128)} %constant.71) | copy-start | bytes 388
  117.4 72.2 %all-to-all-start = ((bf16[64,8,192]{2,0,1:T(8,128)(2,1)}), bf16[64,8,192]{2,0,1:T(8,128)(2,1)}, u32[]{:S(2)}, u32[]{:S(2)}) async-start(bf16[64,8,192]{2,0,1:T(8,128)(2,1)} %copy.13), calls=%async_computation.2 | async-start | bytes 524288 | tf_op jit(solution)/shard_map/all_to_all | solution.py:53
  122.0 107.4 %all-reduce.6.cloned.1.call-start = ((), (), s32[]{:S(2)}) async-start(), calls=%async_computation.5 | async-start | bytes 589824 | tf_op jit(solution)/shard_map/psum | solution.py:76
Sparse Core Ops, SparseCore 0:
  60.3 24.7 reduce-scatter.2
  114.9 41.0 reduce-scatter.4
  160.2 41.8 all-reduce.5
where the time goes:
time: 239 us; the launch traced here: 238 us
  blocking collectives  79.9 us (33%)
  other arithmetic  61 us (26%)
  local copies, waits for them, and re-layouts  30.4 us (13%)
  waiting for transfers between devices  24.7 us (10%)
  matrix products  22.2 us (9%)
  between operations  14.5 us (6%)
  starting transfers between devices  4.89 us (2%)
    reduce_sum x2, other arithmetic, slot_table(): return jnp.sum(jnp.where(match, values_rows[:, :, None], 0.0), axis=1)  37.6 us
    unnamed x1, blocking collectives  27.6 us
    reduce_scatter x1, waiting for transfers between devices, shards(): lax.psum_scatter(grad_part, 'leaf', scatter_dimension=0, tiled=True)  24.7 us
    all_gather x1, blocking collectives, shards(): all_coef = lax.all_gather(coef, 'dp', axis=0, tiled=True)  16.8 us
    all_gather x1, blocking collectives, shards(): all_slot = lax.all_gather(local_slot, 'dp', axis=0, tiled=True)  15.8 us
    mul x2, local copies, waits for them, and re-layouts, shards(): (emb_grad / P_SIZE)[:, None, :] * slope  15.2 us
    dot_general x1, matrix products, shards(): jnp.dot(features, head_weight, preferred_element_type=jnp.float32)  11.9 us
    all_gather x1, blocking collectives, shards(): grouped = lax.all_gather(embedded, 'leaf', axis=0, tiled=True)  10.2 us
  transfers between devices with their start and end apart: 4, of which 1 were waited for; matrix products, arithmetic and copies ran while one was open for 16% of the time, Pallas kernels for 0%

commit v1 on v0

--- a/solution.py
+++ b/solution.py
@@ -51,7 +51,21 @@
         jnp.bfloat16
     )
     columns = lax.all_to_all(grouped, "dp", split_axis=1, concat_axis=0, tiled=True)
-    all_coef = lax.all_gather(coef, "dp", axis=0, tiled=True)
+
+    def cover_set(page):
+        how_many = lax.psum(1, "dp")
+        bank = [page]
+        rr = 1
+        while rr < how_many:
+            arr_out = lax.ppermute(
+                bank[rr - 1], "dp", [(dev, (dev - 1) % how_many) for dev in range(how_many)]
+            )
+            bank.append(arr_out)
+            rr += 1
+        seen_now = jnp.concatenate(bank, 0)
+        return jnp.roll(seen_now, lax.axis_index("dp") * page.shape[0], axis=0)
+
+    all_coef = cover_set(coef)
     all_slot = lax.all_gather(local_slot, "dp", axis=0, tiled=True)
     every_pair = jnp.ones(all_slot.shape, jnp.bool_)
     all_table = slot_table(all_slot, every_pair, all_coef.astype(jnp.float32), slots_dev).astype(

time: 239 us -> 267 us (1.12)
  starting transfers between devices: 4.89 us -> 25.5 us
  local copies, waits for them, and re-layouts: 30.4 us -> 40.1 us
  blocking collectives: 79.9 us -> 71.2 us
  waiting for transfers between devices: 24.7 us -> 29.8 us
    ppermute x0 -> x7, starting transfers between devices: none -> 21.1 us  [cover_set(): lax.ppermute(bank[rr - 1], 'dp', [(dev, (dev - 1) % how_many) for dev in...]
    all_gather x1 -> x0, blocking collectives: 16.8 us -> none  [shards(): all_coef = lax.all_gather(coef, 'dp', axis=0, tiled=True)]
    unnamed x18 -> x33, local copies, waits for them, and re-layouts: 2.46 us -> 11.6 us
    all_gather x1, blocking collectives: 15.8 us -> 22.1 us  [shards(): all_slot = lax.all_gather(local_slot, 'dp', axis=0, tiled=True)]
    ppermute x0 -> x7, waiting for transfers between devices: none -> 5.02 us  [cover_set(): lax.ppermute(bank[rr - 1], 'dp', [(dev, (dev - 1) % how_many) for dev in...]
  transfers between devices with their start and end apart: 4 -> 11, of which waited for: 1 -> 7; matrix products, arithmetic and copies ran while one was open for 16% -> 19% of each run, Pallas kernels for 0% -> 0%
where the time goes in v1:
time: 267 us; the launch traced here: 266 us
  blocking collectives  71.2 us (27%)
  other arithmetic  62.7 us (23%)
  local copies, waits for them, and re-layouts  40.1 us (15%)
  waiting for transfers between devices  29.8 us (11%)
  starting transfers between devices  25.5 us (10%)
  matrix products  22.2 us (8%)
  between operations  14.6 us (5%)
    reduce_sum x2, other arithmetic, slot_table(): return jnp.sum(jnp.where(match, values_rows[:, :, None], 0.0), axis=1)  37.6 us
    unnamed x1, blocking collectives  29.3 us
    reduce_scatter x1, waiting for transfers between devices, shards(): lax.psum_scatter(grad_part, 'leaf', scatter_dimension=0, tiled=True)  24.7 us
    all_gather x1, blocking collectives, shards(): all_slot = lax.all_gather(local_slot, 'dp', axis=0, tiled=True)  22.1 us
    ppermute x7, starting transfers between devices, cover_set(): lax.ppermute(bank[rr - 1], 'dp', [(dev, (dev - 1) % how_many) for dev in...  21.1 us
    mul x2, local copies, waits for them, and re-layouts, shards(): (emb_grad / P_SIZE)[:, None, :] * slope  15.2 us
    dot_general x1, matrix products, shards(): jnp.dot(features, head_weight, preferred_element_type=jnp.float32)  11.9 us
    unnamed x33, local copies, waits for them, and re-layouts  11.6 us
  transfers between devices with their start and end apart: 11, of which 7 were waited for; matrix products, arithmetic and copies ran while one was open for 19% of the time, Pallas kernels for 0%

profile of v1, /device:TPU:0, one launch (start us, length us, event | category | flops | bytes accessed | tf_op | source)
XLA Modules:
  0.0 265.9 jit_solution(1800237899603414398)
XLA Ops:
  8.2 11.9 %fusion.1 = (f32[1600,1536]{1,0:T(8,128)}, f32[1600,1536]{1,0:T(8,128)}) fusion(f32[1536]{0:T(1024)} %param.10, f32[1536]{0:T(1024)} %param.9, bf16[1600,384]{1,0:T(8,128)(2,1)} %param.7, bf16[384,1536]{1,0:T(8,128)(2,1)} %param.8), kind=kOutput, calls=%fused_computation.11 | convolution fusion | flops 1902182400 | bytes 22081536 | tf_op jit(solution)/shard_map/dot_general | solution.py:20
  20.1 10.0 %reshape.27 = f32[16,100,1536]{2,1,0:T(8,128)} reshape(f32[1600,1536]{1,0:T(8,128)} %get-tuple-element.15) | data formatting | bytes 19660800 | tf_op jit(solution)/shard_map/reshape | solution.py:24
  30.1 5.3 %reduce_sum.74 = f32[16,1536]{1,0:T(8,128)S(1)} reduce(f32[16,100,1536]{2,1,0:T(8,128)} %reshape.27, f32[]{:T(128)} %constant.86.clone.1), dimensions={1}, to_apply=%region_2.3 | reduce | flops 2433024 | bytes 9928708 | tf_op jit(solution)/shard_map/reduce_sum | solution.py:24
  35.5 10.2 %all_gather.6 = bf16[64,1536]{1,0:T(8,128)(2,1)S(1)} all-gather(bf16[16,1536]{1,0:T(8,128)(2,1)S(1)} %multiply_convert_fusion.4), channel_id=1, replica_groups=mesh['dp'=8,'leaf'=4] {'leaf'}, dimensions={0}, use_global_device_ids=true | all-gather | bytes 245760 | tf_op jit(solution)/shard_map/all_gather | solution.py:25
  45.6 1.8 select_reduce_fusion.4
  47.6 9.4 %select_reduce_fusion.3 = (f32[64,1024]{1,0:T(8,128)S(1)}, f32[64,1024]{1,0:T(8,128)S(1)}) fusion(s32[64,64]{1,0:T(8,128)S(1)} %get-tuple-element.13, pred[64,64]{1,0:T(8,128)(4,1)S(1)} %get-tuple-element.14, f32[64]{0:T(128)S(1)} %compare_convert_fusion), kind=kLoop, calls=%fused_computation.4 | loop fusion | flops 25034752 | bytes 545024 | tf_op jit(solution)/shard_map/reduce_sum | solution.py:14
  60.4 24.7 %reduce-scatter.3.cloned.1.call-done = f32[16,1536]{1,0:T(8,128)} async-done(((f32[64,1536]{1,0:T(8,128)}), f32[16,1536]{1,0:T(8,128)}) %reduce-scatter.3.cloned.1.call-update) | async-done | bytes 98320 | tf_op jit(solution)/shard_map/reduce_scatter | solution.py:47
  86.0 5.2 %mul.48 = f32[16,100,1536]{2,1,0:T(8,128)} broadcast(f32[16,1536]{1,0:T(8,128)S(1)} %broadcast_multiply_fusion), dimensions={0,2} | broadcast | bytes 9928704 | tf_op jit(solution)/shard_map/mul | solution.py:78
  91.2 10.0 %mul.49 = f32[1600,1536]{1,0:T(8,128)} reshape(f32[16,100,1536]{2,1,0:T(8,128)} %mul.48) | data formatting | bytes 19660800 | tf_op jit(solution)/shard_map/mul | solution.py:78
  101.2 9.0 %fusion.20 = (f32[1536]{0:T(1024)S(1)}, f32[1536]{0:T(1024)S(1)}, f32[1600,1536]{1,0:T(8,128)S(1)}) fusion(f32[1600,1536]{1,0:T(8,128)} %get-tuple-element.16, f32[1600,1536]{1,0:T(8,128)} %mul.49, f32[1536]{0:T(1024)S(1)} %copy-done.2, f32[1536]{0:T(1024)S(1)} %copy-done.3), kind=kLoop, calls=%fused_computation.69 | loop fusion | flops 31945728 | bytes 29515776 | tf_op jit(solution)/shard_map/reduce_sum | solution.py:84
  110.3 4.5 %fusion.4 = f32[384,1536]{0,1:T(8,128)} fusion(bf16[1600,384]{1,0:T(8,128)(2,1)S(1)} %copy-done.5, f32[1600,1536]{1,0:T(8,128)S(1)} %get-tuple-element.12, f32[1536]{0:T(1024)S(1)} %copy-done.3), kind=kOutput, calls=%fused_computation.15 | convolution fusion | flops 1892352000 | bytes 13424640 | tf_op jit(solution)/shard_map/dot_general | solution.py:80
  114.8 5.3 %select_reduce_fusion.1 = bf16[64,64]{1,0:T(8,128)(2,1)S(1)} fusion(f32[64,1024]{1,0:T(8,128)} %get-tuple-element.17, s32[64,64]{1,0:T(8,128)S(1)} %get-tuple-element.13, pred[64,64]{1,0:T(8,128)(4,1)S(1)} %get-tuple-element.14), kind=kLoop, calls=%fused_computation.2 | loop fusion | flops 16773120 | bytes 290816 | tf_op jit(solution)/shard_map/reduce_sum | solution.py:50
  120.1 2.5 collective-permute-start
  125.2 4.0 %all-to-all-start = ((bf16[64,8,192]{2,0,1:T(8,128)(2,1)}), bf16[64,8,192]{2,0,1:T(8,128)(2,1)}, u32[]{:S(2)}, u32[]{:S(2)}) async-start(bf16[64,8,192]{2,0,1:T(8,128)(2,1)} %copy.13), calls=%async_computation.2 | async-start | bytes 524288 | tf_op jit(solution)/shard_map/all_to_all | solution.py:53
  130.0 22.1 %all_gather.7 = s32[512,64]{1,0:T(8,128)S(1)} all-gather(s32[64,64]{1,0:T(8,128)S(1)} %get-tuple-element.13), channel_id=1, replica_groups=mesh['dp'=8,'leaf'=4] {'dp'}, dimensions={0}, use_global_device_ids=true | all-gather | bytes 147456 | tf_op jit(solution)/shard_map/all_gather | solution.py:69
  155.8 3.5 %collective-permute-start.2 = (bf16[64,64]{1,0:T(8,128)(2,1)S(1)}, bf16[64,64]{1,0:T(8,128)(2,1)S(1)}, u32[]{:S(2)}, u32[]{:S(2)}) collective-permute-start(bf16[64,64]{1,0:T(8,128)(2,1)S(1)} %collective-permute-done.1), channel_id=1, source_target_pairs={{0,28},{4,0},{8,4},{12,8},{16,12},{20,16},{24,20},{28,24},{1,29},{... | collective-permute-start | bytes 24584 | tf_op jit(solution)/shard_map/ppermute | solution.py:60
  160.8 3.5 %collective-permute-start.3 = (bf16[64,64]{1,0:T(8,128)(2,1)S(1)}, bf16[64,64]{1,0:T(8,128)(2,1)S(1)}, u32[]{:S(2)}, u32[]{:S(2)}) collective-permute-start(bf16[64,64]{1,0:T(8,128)(2,1)S(1)} %collective-permute-done.2), channel_id=1, source_target_pairs={{0,28},{4,0},{8,4},{12,8},{16,12},{20,16},{24,20},{28,24},{1,29},{... | collective-permute-start | bytes 24584 | tf_op jit(solution)/shard_map/ppermute | solution.py:60
  165.7 3.5 %collective-permute-start.4 = (bf16[64,64]{1,0:T(8,128)(2,1)S(1)}, bf16[64,64]{1,0:T(8,128)(2,1)S(1)}, u32[]{:S(2)}, u32[]{:S(2)}) collective-permute-start(bf16[64,64]{1,0:T(8,128)(2,1)S(1)} %collective-permute-done.3), channel_id=1, source_target_pairs={{0,28},{4,0},{8,4},{12,8},{16,12},{20,16},{24,20},{28,24},{1,29},{... | collective-permute-start | bytes 24584 | tf_op jit(solution)/shard_map/ppermute | solution.py:60
  170.7 3.5 %collective-permute-start.5 = (bf16[64,64]{1,0:T(8,128)(2,1)S(1)}, bf16[64,64]{1,0:T(8,128)(2,1)S(1)}, u32[]{:S(2)}, u32[]{:S(2)}) collective-permute-start(bf16[64,64]{1,0:T(8,128)(2,1)S(1)} %collective-permute-done.4), channel_id=1, source_target_pairs={{0,28},{4,0},{8,4},{12,8},{16,12},{20,16},{24,20},{28,24},{1,29},{... | collective-permute-start | bytes 24584 | tf_op jit(solution)/shard_map/ppermute | solution.py:60
  175.7 3.5 %collective-permute-start.6 = (bf16[64,64]{1,0:T(8,128)(2,1)S(1)}, bf16[64,64]{1,0:T(8,128)(2,1)S(1)}, u32[]{:S(2)}, u32[]{:S(2)}) collective-permute-start(bf16[64,64]{1,0:T(8,128)(2,1)S(1)} %collective-permute-done.5), channel_id=1, source_target_pairs={{0,28},{4,0},{8,4},{12,8},{16,12},{20,16},{24,20},{28,24},{1,29},{... | collective-permute-start | bytes 24584 | tf_op jit(solution)/shard_map/ppermute | solution.py:60
  187.7 28.3 %select_reduce_fusion = bf16[512,1024]{1,0:T(8,128)(2,1)} fusion(f32[512,64]{1,0:T(8,128)} %dynamic-slice_convert_fusion, s32[512,64]{1,0:T(8,128)S(1)} %all_gather.7), kind=kLoop, calls=%fused_computation | loop fusion | flops 100139008 | bytes 1310720 | tf_op jit(solution)/shard_map/reduce_sum | solution.py:14
  216.0 2.6 fusion.23
  218.6 29.3 %all-reduce.2 = (f32[1536]{0:T(1024)S(1)}, f32[1536]{0:T(1024)S(1)}) all-reduce(f32[1536]{0:T(1024)S(1)} %get-tuple-element.5, f32[1536]{0:T(1024)S(1)} %get-tuple-element.4), channel_id=4, replica_groups=mesh['dp'=8,'leaf'=4] {'dp'}, use_global_device_ids=true, to_apply=%region_8.9.clone | all-reduce | flops 3072 | bytes 24576
  248.0 9.7 %all-reduce.3 = (f32[192]{0:T(256)}, f32[192]{0:T(256)}) all-reduce(f32[192]{0:T(256)S(1)} %dynamic-slice.1, f32[192]{0:T(256)S(1)} %dynamic-slice.3), channel_id=1, replica_groups=mesh['dp'=8,'leaf'=4] {'leaf'}, use_global_device_ids=true, to_apply=%region_9.10 | all-reduce | flops 384 | bytes 3072 | tf_op jit(solution)/shard_map/psum | solution.py:90
  (61 shorter events, 28.0 us)
Async XLA Ops:
  7.2 49.8 %copy-start = (bf16[1024,1536]{1,0:T(8,128)(2,1)S(1)}, bf16[1024,1536]{1,0:T(8,128)(2,1)}, u32[]{:S(2)}) copy-start(bf16[1024,1536]{1,0:T(8,128)(2,1)} %param.11) | copy-start | bytes 9437188
  7.2 77.9 %reduce-scatter.3.cloned.1.call-start = ((), (), s32[]{:S(2)}) async-start(), calls=%async_computation.3 | async-start | bytes 491520 | tf_op jit(solution)/shard_map/reduce_scatter | solution.py:47
  30.1 15.5 %copy-start.4 = (s32[64]{0:T(128)S(1)}, s32[64]{0:T(128)}, u32[]{:S(2)}) copy-start(s32[64]{0:T(128)} %param.12) | copy-start | bytes 772
  30.1 17.3 %copy-start.1 = (s32[64,64]{1,0:T(8,128)S(1)}, s32[64,64]{1,0:T(8,128)}, u32[]{:S(2)}) copy-start(s32[64,64]{1,0:T(8,128)} %param.13) | copy-start | bytes 49156
  60.2 127.5 %reduce-scatter.5.cloned.1.call-start = ((), (), s32[]{:S(2)}) async-start(), calls=%async_computation.4 | async-start | bytes 2654208 | tf_op jit(solution)/shard_map/reduce_scatter | solution.py:86
  91.1 10.1 %copy-start.2 = (f32[1536]{0:T(1024)S(1)}, f32[1536]{0:T(1024)}, u32[]{:S(2)}) copy-start(f32[1536]{0:T(1024)} %param.10) | copy-start | bytes 18436
  91.2 10.1 %copy-start.3 = (f32[1536]{0:T(1024)S(1)}, f32[1536]{0:T(1024)}, u32[]{:S(2)}) copy-start(f32[1536]{0:T(1024)} %param.9) | copy-start | bytes 18436
  101.2 9.0 %copy-start.5 = (bf16[1600,384]{1,0:T(8,128)(2,1)S(1)}, bf16[1600,384]{1,0:T(8,128)(2,1)}, u32[]{:S(2)}) copy-start(bf16[1600,384]{1,0:T(8,128)(2,1)} %param.7) | copy-start | bytes 3686404
  110.3 41.8 %copy-start.6 = (u32[32]{0:T(128)S(1)}, u32[32]{0:T(128)}, u32[]{:S(2)}) copy-start(u32[32]{0:T(128)} %constant.97) | copy-start | bytes 388
  120.1 33.2 %collective-permute-start = (bf16[64,64]{1,0:T(8,128)(2,1)S(1)}, bf16[64,64]{1,0:T(8,128)(2,1)S(1)}, u32[]{:S(2)}, u32[]{:S(2)}) collective-permute-start(bf16[64,64]{1,0:T(8,128)(2,1)S(1)} %select_reduce_fusion.1), channel_id=1, source_target_pairs={{0,28},{4,0},{8,4},{12,8},{16,12},{20,16},{24,20},{28,24},{1,29},{... | collective-permute-start | bytes 24584 | tf_op jit(solution)/shard_map/ppermute | solution.py:60
  125.2 90.8 %all-to-all-start = ((bf16[64,8,192]{2,0,1:T(8,128)(2,1)}), bf16[64,8,192]{2,0,1:T(8,128)(2,1)}, u32[]{:S(2)}, u32[]{:S(2)}) async-start(bf16[64,8,192]{2,0,1:T(8,128)(2,1)} %copy.13), calls=%async_computation.2 | async-start | bytes 524288 | tf_op jit(solution)/shard_map/all_to_all | solution.py:53
  129.3 128.4 %all-reduce.6.cloned.1.call-start = ((), (), s32[]{:S(2)}) async-start(), calls=%async_computation.5 | async-start | bytes 589824 | tf_op jit(solution)/shard_map/psum | solution.py:90
  153.3 2.5 collective-permute-start.1
  155.8 5.0 %collective-permute-start.2 = (bf16[64,64]{1,0:T(8,128)(2,1)S(1)}, bf16[64,64]{1,0:T(8,128)(2,1)S(1)}, u32[]{:S(2)}, u32[]{:S(2)}) collective-permute-start(bf16[64,64]{1,0:T(8,128)(2,1)S(1)} %collective-permute-done.1), channel_id=1, source_target_pairs={{0,28},{4,0},{8,4},{12,8},{16,12},{20,16},{24,20},{28,24},{1,29},{... | collective-permute-start | bytes 24584 | tf_op jit(solution)/shard_map/ppermute | solution.py:60
  160.8 5.0 %collective-permute-start.3 = (bf16[64,64]{1,0:T(8,128)(2,1)S(1)}, bf16[64,64]{1,0:T(8,128)(2,1)S(1)}, u32[]{:S(2)}, u32[]{:S(2)}) collective-permute-start(bf16[64,64]{1,0:T(8,128)(2,1)S(1)} %collective-permute-done.2), channel_id=1, source_target_pairs={{0,28},{4,0},{8,4},{12,8},{16,12},{20,16},{24,20},{28,24},{1,29},{... | collective-permute-start | bytes 24584 | tf_op jit(solution)/shard_map/ppermute | solution.py:60
  165.7 5.0 %collective-permute-start.4 = (bf16[64,64]{1,0:T(8,128)(2,1)S(1)}, bf16[64,64]{1,0:T(8,128)(2,1)S(1)}, u32[]{:S(2)}, u32[]{:S(2)}) collective-permute-start(bf16[64,64]{1,0:T(8,128)(2,1)S(1)} %collective-permute-done.3), channel_id=1, source_target_pairs={{0,28},{4,0},{8,4},{12,8},{16,12},{20,16},{24,20},{28,24},{1,29},{... | collective-permute-start | bytes 24584 | tf_op jit(solution)/shard_map/ppermute | solution.py:60
  170.7 5.0 %collective-permute-start.5 = (bf16[64,64]{1,0:T(8,128)(2,1)S(1)}, bf16[64,64]{1,0:T(8,128)(2,1)S(1)}, u32[]{:S(2)}, u32[]{:S(2)}) collective-permute-start(bf16[64,64]{1,0:T(8,128)(2,1)S(1)} %collective-permute-done.4), channel_id=1, source_target_pairs={{0,28},{4,0},{8,4},{12,8},{16,12},{20,16},{24,20},{28,24},{1,29},{... | collective-permute-start | bytes 24584 | tf_op jit(solution)/shard_map/ppermute | solution.py:60
  175.7 5.0 %collective-permute-start.6 = (bf16[64,64]{1,0:T(8,128)(2,1)S(1)}, bf16[64,64]{1,0:T(8,128)(2,1)S(1)}, u32[]{:S(2)}, u32[]{:S(2)}) collective-permute-start(bf16[64,64]{1,0:T(8,128)(2,1)S(1)} %collective-permute-done.5), channel_id=1, source_target_pairs={{0,28},{4,0},{8,4},{12,8},{16,12},{20,16},{24,20},{28,24},{1,29},{... | collective-permute-start | bytes 24584 | tf_op jit(solution)/shard_map/ppermute | solution.py:60
Sparse Core Ops, SparseCore 0:
  60.3 24.7 reduce-scatter.2
  114.9 41.1 reduce-scatter.4
  187.9 43.7 all-reduce.5
